TPU v7x, 256 devices: a whole 4x4x8 slice. The times are simulated.
256 devices in a mesh: section: 16 (over z_lo, x, core), tp: 16 (over y, z_hi).
Axes of the slice: x: 4, y: 4, z: 8 (z_hi: 4, z_lo: 2; z = z_hi * 2 + z_lo), core: 2. Of those that a mesh axis runs over, the one named last changes fastest.
Arguments:
- tokens: bfloat16 [2, 512, 4096], P(None, 'tp'), may hold values from -6 to 6
- norm_gains: float32 [2, 4096], replicated, may hold values from 0.1 to 1.9
- w_gate: bfloat16 [16, 4096, 2048], P('section', None, 'tp'), may hold values from -0.09375 to 0.09375
- w_up: bfloat16 [16, 4096, 2048], P('section', None, 'tp'), may hold values from -0.09375 to 0.09375
- w_down: bfloat16 [16, 2048, 4096], P('section', 'tp'), may hold values from -0.0625 to 0.0625
Outputs:
- acts: bfloat16 [16, 2, 512, 512], P('section', None, 'tp')
All inputs are finite; a program needn't handle non-finite values.
Results may differ from a plain program's by a relative error of at most 0.022.
Values may be sent and summed in bfloat16 or wider, within the bound.
No kernel may reach another device: no remote copies, remote signals or barrier semaphores. Data moves between devices by JAX's collectives and lax.ppermute only.
A program may use at most 64 MiB of HBM per device.

v0:
```python
import jax
import jax.numpy as jnp
from jax import lax
from jax.sharding import PartitionSpec as P

LAYERS = 2
PIECES = 1
epsilon = 1e-05


def swapped(value, axis, mask):
    pairs = [(source, source ^ mask) for source in range(lax.axis_size(axis))]
    return lax.ppermute(value, axis, pairs)


def shifted(value, axis, steps):
    count = lax.axis_size(axis)
    return lax.ppermute(value, axis, [(source, source + steps) for source in range(count - steps)])


def body(tokens, norm_gains, w_gate, w_up, w_down):
    section_count = lax.axis_size("section")
    split = section_count // LAYERS
    bit_count = split.bit_length() - 1
    position = lax.axis_index("section")
    section_layer = position // split
    member = position % split
    core = member % 2
    xpos = member // 2
    x_count = split // 2
    micro_count, tok_dev, model_width = tokens.shape
    piece_width = model_width // split
    half_width = model_width // 2
    row_count = tok_dev // PIECES
    piece_count = micro_count * PIECES
    tick_count = piece_count + LAYERS - 1

    def pick(value, axis, which):
        shape = value.shape
        grouped = value.reshape(shape[:axis] + (x_count, 2, piece_width) + shape[axis + 1 :])
        chosen = lax.dynamic_index_in_dim(grouped, which, axis + 1, keepdims=False)
        return chosen.reshape(shape[:axis] + (half_width,) + shape[axis + 1 :])

    other = 1 - core
    gate_own = pick(w_gate[0], 0, core)
    gate_other = pick(w_gate[0], 0, other)
    up_own = pick(w_up[0], 0, core)
    up_other = pick(w_up[0], 0, other)
    down_own = pick(w_down[0], 1, core)
    down_other = pick(w_down[0], 1, other)
    norm_gain = lax.dynamic_index_in_dim(norm_gains, section_layer, 0, keepdims=False)
    gain_own = pick(norm_gain, 0, core)

    def from_tokens(piece_index):
        micro_index, part = divmod(piece_index, PIECES)
        rows = tokens[micro_index, part * row_count : (part + 1) * row_count].astype(jnp.float32)
        return (pick(rows, 1, core), jnp.sum(rows * rows, axis=1, keepdims=True))

    def from_received(received):
        current = received.astype(jnp.float32)
        own_sq = jnp.sum(current * current, axis=1, keepdims=True)
        return (current, own_sq + swapped(own_sq, "section", 1))

    def tick(current, square_sum):
        inv_rms = lax.rsqrt(square_sum / model_width + epsilon)
        normed = (current * inv_rms * gain_own).astype(jnp.bfloat16)
        gathered = lax.all_gather(normed, "tp", axis=0, tiled=True)
        gathered_other = swapped(gathered, "section", 1)
        gate_proj = jnp.dot(gathered, gate_own, preferred_element_type=jnp.float32) + jnp.dot(
            gathered_other, gate_other, preferred_element_type=jnp.float32
        )
        up_proj = jnp.dot(gathered, up_own, preferred_element_type=jnp.float32) + jnp.dot(
            gathered_other, up_other, preferred_element_type=jnp.float32
        )
        active = (jax.nn.silu(gate_proj) * up_proj).astype(jnp.bfloat16)
        part_other = jnp.dot(active, down_other, preferred_element_type=jnp.float32).astype(
            jnp.bfloat16
        )
        part_from_other = swapped(part_other, "section", 1)
        part_own = jnp.dot(active, down_own, preferred_element_type=jnp.float32).astype(
            jnp.bfloat16
        )
        pair = (part_own.astype(jnp.float32) + part_from_other.astype(jnp.float32)).astype(
            jnp.bfloat16
        )
        summed = lax.psum_scatter(pair, "tp", scatter_dimension=0, tiled=True)
        for level in range(1, bit_count):
            summed = summed.astype(jnp.float32) + swapped(summed, "section", 1 << level).astype(
                jnp.float32
            )
            if level < bit_count - 1:
                summed = summed.astype(jnp.bfloat16)
        full_half = (current + summed.astype(jnp.float32)).astype(jnp.bfloat16)
        block = lax.dynamic_index_in_dim(
            full_half.reshape(row_count, x_count, piece_width), xpos, 1, keepdims=False
        )
        return (full_half, block)

    blocks = []
    received = None
    for tick_index in range(tick_count):
        if tick_index == 0:
            current, square_sum = from_tokens(0)
        elif tick_index >= piece_count:
            current, square_sum = from_received(received)
        else:
            first_current, first_sum = from_tokens(tick_index)
            later_current, later_sum = from_received(received)
            is_first = section_layer == 0
            current = jnp.where(is_first, first_current, later_current)
            square_sum = jnp.where(is_first, first_sum, later_sum)
        full_half, block = tick(current, square_sum)
        blocks.append(block)
        if tick_index < tick_count - 1:
            received = shifted(full_half, "section", split)
    stacked = jnp.stack(blocks, axis=0)
    outputs = []
    for micro_index in range(micro_count):
        parts = [
            lax.dynamic_index_in_dim(
                stacked, micro_index * PIECES + part + section_layer, 0, keepdims=False
            )
            for part in range(PIECES)
        ]
        outputs.append(jnp.concatenate(parts, axis=0))
    return jnp.stack(outputs, axis=0)[None]


def solution(mesh):
    in_specs = (
        P(None, "tp", None),
        P(),
        P("section", None, "tp"),
        P("section", None, "tp"),
        P("section", "tp", None),
    )
    out_specs = P("section", None, "tp", None)
    return jax.shard_map(body, mesh=mesh, in_specs=in_specs, out_specs=out_specs, check_vma=False)
```

profile of v0, /device:TPU:6, one launch (start us, length us, event | category | flops | bytes accessed | tf_op | source)
XLA Modules:
  0.0 558.7 jit_solution(12921306199294246905)
XLA Ops:
  6.5 1.1 slice_convert_fusion.1
  7.7 1.2 multiply_reduce_fusion
  9.8 1.6 dynamic-slice_reduce_fusion
  11.6 0.7 multiply_convert_fusion.1
  12.4 62.2 %all-gather.4.cloned.1.call-done = bf16[512,2048]{1,0:T(8,128)(2,1)} async-done(((bf16[32,2048]{1,0:T(8,128)(2,1)}), bf16[512,2048]{1,0:T(8,128)(2,1)}) %all-gather.4.cloned.1.call-update) | async-done | bytes 2097168 | tf_op jit(solution)/shard_map/all_gather | solution.py:67
  74.6 1.6 copy.14
  76.3 1.8 constant_dynamic-slice_fusion.7
  80.0 2.3 convolution_add_fusion.5
  82.3 2.3 fusion.3
  85.9 3.8 collective-permute-done.1
  89.7 2.1 add_convert_fusion.2
  91.9 88.2 %reduce-scatter.4.cloned.1.call-done = bf16[32,2048]{1,0:T(8,128)(2,1)} async-done(((bf16[512,2048]{1,0:T(8,128)(2,1)}), bf16[32,2048]{1,0:T(8,128)(2,1)}) %reduce-scatter.4.cloned.1.call-update) | async-done | bytes 131088 | tf_op jit(solution)/shard_map/reduce_scatter | solution.py:86
  180.0 0.8 collective-permute-start.2
  180.8 4.9 collective-permute-done.2
  185.8 0.9 add_convert_fusion.7
  186.7 0.9 collective-permute-start.3
  187.6 5.6 %collective-permute-done.3 = bf16[32,2048]{1,0:T(8,128)(2,1)S(1)} collective-permute-done((bf16[32,2048]{1,0:T(8,128)(2,1)S(1)}, bf16[32,2048]{1,0:T(8,128)(2,1)S(1)}, u32[]{:S(2)}, u32[]{:S(2)}) %collective-permute-start.3) | collective-permute-done | bytes 131104 | tf_op jit(solution)/shard_map/ppermute | solution.py:13
  193.3 1.6 collective-permute-start.4
  194.9 2.5 collective-permute-done.4
  197.7 1.1 collective-permute-done.5
  198.8 0.7 multiply_convert_fusion
  199.6 58.4 %all-gather.6.cloned.1.call-done = bf16[512,2048]{1,0:T(8,128)(2,1)} async-done(((bf16[32,2048]{1,0:T(8,128)(2,1)}), bf16[512,2048]{1,0:T(8,128)(2,1)}) %all-gather.6.cloned.1.call-update) | async-done | bytes 2097168 | tf_op jit(solution)/shard_map/all_gather | solution.py:67
  258.0 2.4 fusion.15
  261.1 1.2 collective-permute-done.6
  263.1 0.7 fusion.4
  264.7 4.0 collective-permute-done.7
  268.7 2.1 add_convert_fusion.1
  270.9 88.1 %reduce-scatter.6.cloned.1.call-done = bf16[32,2048]{1,0:T(8,128)(2,1)} async-done(((bf16[512,2048]{1,0:T(8,128)(2,1)}), bf16[32,2048]{1,0:T(8,128)(2,1)}) %reduce-scatter.6.cloned.1.call-update) | async-done | bytes 131088 | tf_op jit(solution)/shard_map/reduce_scatter | solution.py:86
  358.9 0.9 collective-permute-start.8
  359.8 4.8 collective-permute-done.8
  364.6 0.9 add_convert_fusion.5
  365.5 1.1 collective-permute-start.9
  366.6 5.5 collective-permute-done.9
  372.1 1.7 collective-permute-start.10
  373.8 2.5 collective-permute-done.10
  376.6 1.1 collective-permute-done.11
  377.7 0.8 fusion.9
  378.5 58.4 %all-gather.8.cloned.1.call-done = bf16[512,2048]{1,0:T(8,128)(2,1)} async-done(((bf16[32,2048]{1,0:T(8,128)(2,1)}), bf16[512,2048]{1,0:T(8,128)(2,1)}) %all-gather.8.cloned.1.call-update) | async-done | bytes 2097168 | tf_op jit(solution)/shard_map/all_gather | solution.py:67
  436.9 2.5 fusion.17
  440.1 1.2 collective-permute-done.12
  443.7 4.0 collective-permute-done.13
  447.7 2.1 add_convert_fusion
  449.8 88.1 %reduce-scatter.8.cloned.1.call-done = bf16[32,2048]{1,0:T(8,128)(2,1)} async-done(((bf16[512,2048]{1,0:T(8,128)(2,1)}), bf16[32,2048]{1,0:T(8,128)(2,1)}) %reduce-scatter.8.cloned.1.call-update) | async-done | bytes 131088 | tf_op jit(solution)/shard_map/reduce_scatter | solution.py:86
  537.8 0.9 collective-permute-start.14
  538.8 4.7 collective-permute-done.14
  543.5 0.9 add_convert_fusion.3
  544.4 1.1 collective-permute-start.15
  545.8 5.2 collective-permute-done.15
  (73 shorter events, 11.8 us)
Async XLA Ops:
  6.5 4.9 copy-start
  6.5 68.1 %all-gather.4.cloned.1.call-start = ((), (), s32[]{:S(2)}) async-start(), calls=%async_computation.3 | async-start | bytes 2228224 | tf_op jit(solution)/shard_map/all_gather | solution.py:67
  12.4 167.7 %reduce-scatter.4.cloned.1.call-start = ((), (), s32[]{:S(2)}) async-start(), calls=%async_computation.4 | async-start | bytes 2228224 | tf_op jit(solution)/shard_map/reduce_scatter | solution.py:86
  74.6 5.4 collective-permute-start
  76.3 2.2 copy-start.1
  78.2 4.1 copy-start.4
  85.3 4.4 collective-permute-start.1
  91.8 166.2 %all-gather.6.cloned.1.call-start = ((), (), s32[]{:S(2)}) async-start(), calls=%async_computation.5 | async-start | bytes 2228224 | tf_op jit(solution)/shard_map/all_gather | solution.py:67
  180.0 5.7 %collective-permute-start.2 = (bf16[32,2048]{1,0:T(8,128)(2,1)}, bf16[32,2048]{1,0:T(8,128)(2,1)S(1)}, u32[]{:S(2)}, u32[]{:S(2)}) collective-permute-start(bf16[32,2048]{1,0:T(8,128)(2,1)} %reduce-scatter.4.cloned.1.call-done), channel_id=1, source_target_pairs={{0,32},{16,48},{32,0},{48,16},{64,96},{80,112},{96,64},{112,80},{1... | collective-permute-start | bytes 393224 | tf_op jit(solution)/shard_map/ppermute | solution.py:13
  186.7 6.6 %collective-permute-start.3 = (bf16[32,2048]{1,0:T(8,128)(2,1)S(1)}, bf16[32,2048]{1,0:T(8,128)(2,1)S(1)}, u32[]{:S(2)}, u32[]{:S(2)}) collective-permute-start(bf16[32,2048]{1,0:T(8,128)(2,1)S(1)} %add_convert_fusion.7), channel_id=1, source_target_pairs={{0,64},{16,80},{32,96},{48,112},{64,0},{80,16},{96,32},{112,48},{1... | collective-permute-start | bytes 393224 | tf_op jit(solution)/shard_map/ppermute | solution.py:13
  193.3 4.1 collective-permute-start.4
  197.5 1.2 collective-permute-start.5
  199.5 159.4 %reduce-scatter.6.cloned.1.call-start = ((), (), s32[]{:S(2)}) async-start(), calls=%async_computation.6 | async-start | bytes 2228224 | tf_op jit(solution)/shard_map/reduce_scatter | solution.py:86
  258.0 2.5 copy-start.3
  258.0 4.4 collective-permute-start.6
  261.1 1.9 copy-start.5
  264.5 4.2 collective-permute-start.7
  270.8 166.1 %all-gather.8.cloned.1.call-start = ((), (), s32[]{:S(2)}) async-start(), calls=%async_computation.7 | async-start | bytes 2228224 | tf_op jit(solution)/shard_map/all_gather | solution.py:67
  358.9 5.6 %collective-permute-start.8 = (bf16[32,2048]{1,0:T(8,128)(2,1)}, bf16[32,2048]{1,0:T(8,128)(2,1)S(1)}, u32[]{:S(2)}, u32[]{:S(2)}) collective-permute-start(bf16[32,2048]{1,0:T(8,128)(2,1)} %reduce-scatter.6.cloned.1.call-done), channel_id=1, source_target_pairs={{0,32},{16,48},{32,0},{48,16},{64,96},{80,112},{96,64},{112,80},{1... | collective-permute-start | bytes 393224 | tf_op jit(solution)/shard_map/ppermute | solution.py:13
  365.5 6.6 %collective-permute-start.9 = (bf16[32,2048]{1,0:T(8,128)(2,1)S(1)}, bf16[32,2048]{1,0:T(8,128)(2,1)S(1)}, u32[]{:S(2)}, u32[]{:S(2)}) collective-permute-start(bf16[32,2048]{1,0:T(8,128)(2,1)S(1)} %add_convert_fusion.5), channel_id=1, source_target_pairs={{0,64},{16,80},{32,96},{48,112},{64,0},{80,16},{96,32},{112,48},{1... | collective-permute-start | bytes 393224 | tf_op jit(solution)/shard_map/ppermute | solution.py:13
  372.1 4.2 collective-permute-start.10
  376.5 1.2 collective-permute-start.11
  378.5 159.3 %reduce-scatter.8.cloned.1.call-start = ((), (), s32[]{:S(2)}) async-start(), calls=%async_computation.8 | async-start | bytes 2228224 | tf_op jit(solution)/shard_map/reduce_scatter | solution.py:86
  436.9 2.5 copy-start.2
  436.9 4.4 collective-permute-start.12
  440.1 1.9 copy-start.6
  443.5 4.2 collective-permute-start.13
  537.8 5.6 %collective-permute-start.14 = (bf16[32,2048]{1,0:T(8,128)(2,1)}, bf16[32,2048]{1,0:T(8,128)(2,1)S(1)}, u32[]{:S(2)}, u32[]{:S(2)}) collective-permute-start(bf16[32,2048]{1,0:T(8,128)(2,1)} %reduce-scatter.8.cloned.1.call-done), channel_id=1, source_target_pairs={{0,32},{16,48},{32,0},{48,16},{64,96},{80,112},{96,64},{112,80},{1... | collective-permute-start | bytes 393224 | tf_op jit(solution)/shard_map/ppermute | solution.py:13
  544.4 6.6 %collective-permute-start.15 = (bf16[32,2048]{1,0:T(8,128)(2,1)S(1)}, bf16[32,2048]{1,0:T(8,128)(2,1)S(1)}, u32[]{:S(2)}, u32[]{:S(2)}) collective-permute-start(bf16[32,2048]{1,0:T(8,128)(2,1)S(1)} %add_convert_fusion.3), channel_id=1, source_target_pairs={{0,64},{16,80},{32,96},{48,112},{64,0},{80,16},{96,32},{112,48},{1... | collective-permute-start | bytes 393224 | tf_op jit(solution)/shard_map/ppermute | solution.py:13
Sparse Core Ops, SparseCore 0:
  12.5 62.0 all-gather.3
  91.9 88.0 reduce-scatter.3
  199.6 58.2 all-gather.5
  270.9 87.9 reduce-scatter.5
  378.6 58.2 all-gather.7
  449.9 87.8 reduce-scatter.7
where the time goes:
time: 559 us
  waiting for transfers between devices  495 us (89%)
  matrix products  23.5 us (4%)
  between operations  13.9 us (2%)
  starting transfers between devices  10.3 us (2%)
  other arithmetic  8.52 us (2%)
  local copies, waits for them, and re-layouts  7.12 us (1%)
    reduce_scatter x3, waiting for transfers between devices, tick(): summed = lax.psum_scatter(pair, 'tp', scatter_dimension=0, tiled=True)  264 us
    all_gather x3, waiting for transfers between devices, tick(): gathered = lax.all_gather(normed, 'tp', axis=0, tiled=True)  179 us
    ppermute x14, waiting for transfers between devices, swapped(): return lax.ppermute(value, axis, pairs)  47 us
  transfers between devices with their start and end apart: 22, of which 21 were waited for; matrix products, arithmetic and copies ran while one was open for 2% of the time, Pallas kernels for 0%

commit v1 on v0

--- a/solution.py
+++ b/solution.py
@@ -62,9 +62,18 @@
         return (current, own_sq + swapped(own_sq, "section", 1))
 
     def tick(current, square_sum):
+
+        def heaps_choose(page):
+            return jnp.concatenate(
+                lax.all_to_all(
+                    jnp.stack([page] * lax.axis_size("tp")), "tp", split_axis=0, concat_axis=0
+                ),
+                0,
+            )
+
         inv_rms = lax.rsqrt(square_sum / model_width + epsilon)
         normed = (current * inv_rms * gain_own).astype(jnp.bfloat16)
-        gathered = lax.all_gather(normed, "tp", axis=0, tiled=True)
+        gathered = heaps_choose(normed)
         gathered_other = swapped(gathered, "section", 1)
         gate_proj = jnp.dot(gathered, gate_own, preferred_element_type=jnp.float32) + jnp.dot(
             gathered_other, gate_other, preferred_element_type=jnp.float32

time: 559 us -> 554 us (level)
  waiting for transfers between devices: 495 us -> 333 us
  blocking collectives: 0 us -> 159 us
    all_gather x3 -> x0, waiting for transfers between devices: 179 us -> none  [tick(): gathered = lax.all_gather(normed, 'tp', axis=0, tiled=True)]
    all_to_all x0 -> x3, blocking collectives: none -> 159 us  [heaps_choose(): lax.all_to_all(jnp.stack([page] * lax.axis_size('tp')), 'tp', split_axis=...]
    reduce_scatter x3, waiting for transfers between devices: 264 us -> 279 us  [tick(): summed = lax.psum_scatter(pair, 'tp', scatter_dimension=0, tiled=True)]
  transfers between devices with their start and end apart: 22 -> 19, of which waited for: 21 -> 18; matrix products, arithmetic and copies ran while one was open for 2% -> 2% of each run, Pallas kernels for 0% -> 0%
where the time goes in v1:
time: 554 us; the launch traced here: 553 us
  waiting for transfers between devices  333 us (60%)
  blocking collectives  159 us (29%)
  matrix products  20 us (4%)
  between operations  13.6 us (2%)
  local copies, waits for them, and re-layouts  10.3 us (2%)
  starting transfers between devices  10.3 us (2%)
  other arithmetic  6.56 us (1%)
    reduce_scatter x3, waiting for transfers between devices, tick(): summed = lax.psum_scatter(pair, 'tp', scatter_dimension=0, tiled=True)  279 us
    all_to_all x3, blocking collectives, heaps_choose(): lax.all_to_all(jnp.stack([page] * lax.axis_size('tp')), 'tp', split_axis=...  159 us
    ppermute x14, waiting for transfers between devices, swapped(): return lax.ppermute(value, axis, pairs)  49.4 us
  transfers between devices with their start and end apart: 19, of which 18 were waited for; matrix products, arithmetic and copies ran while one was open for 2% of the time, Pallas kernels for 0%

profile of v1, /device:TPU:6, one launch (start us, length us, event | category | flops | bytes accessed | tf_op | source)
XLA Modules:
  0.0 553.2 jit_solution(9434007852240045671)
XLA Ops:
  6.5 1.1 slice_convert_fusion.1
  7.7 1.2 multiply_reduce_fusion
  9.8 2.2 dynamic-slice_reduce_fusion
  12.6 61.2 %all_to_all.15 = bf16[16,32,2048]{2,1,0:T(8,128)(2,1)S(1)} all-to-all(bf16[16,32,2048]{2,1,0:T(8,128)(2,1)S(1)} %stack.16), channel_id=1, replica_groups=mesh['section'=16,'tp'=16] {'tp'}, dimensions={0} | all-to-all | bytes 4194304 | tf_op jit(solution)/shard_map/all_to_all | solution.py:68
  73.8 1.3 copy.14
  75.1 1.3 constant_dynamic-slice_fusion.6
  76.4 1.9 constant_dynamic-slice_fusion.7
  78.3 0.7 fusion.13
  79.0 0.7 fusion.14
  79.8 2.3 convolution_add_fusion.5
  82.1 2.3 fusion.3
  85.8 3.8 collective-permute-done.1
  89.5 2.1 add_convert_fusion.2
  91.7 87.7 %reduce-scatter.4.cloned.1.call-done = bf16[32,2048]{1,0:T(8,128)(2,1)} async-done(((bf16[512,2048]{1,0:T(8,128)(2,1)}), bf16[32,2048]{1,0:T(8,128)(2,1)}) %reduce-scatter.4.cloned.1.call-update) | async-done | bytes 131088 | tf_op jit(solution)/shard_map/reduce_scatter | solution.py:95
  179.4 0.8 collective-permute-start.2
  180.2 4.9 collective-permute-done.2
  185.0 0.9 add_convert_fusion.7
  186.0 1.0 collective-permute-start.3
  187.0 5.5 %collective-permute-done.3 = bf16[32,2048]{1,0:T(8,128)(2,1)S(1)} collective-permute-done((bf16[32,2048]{1,0:T(8,128)(2,1)S(1)}, bf16[32,2048]{1,0:T(8,128)(2,1)S(1)}, u32[]{:S(2)}, u32[]{:S(2)}) %collective-permute-start.3) | collective-permute-done | bytes 131104 | tf_op jit(solution)/shard_map/ppermute | solution.py:13
  192.6 1.6 collective-permute-start.4
  194.2 2.5 collective-permute-done.4
  197.0 1.0 collective-permute-done.5
  198.4 49.0 %all_to_all.16 = bf16[16,32,2048]{2,1,0:T(8,128)(2,1)S(1)} all-to-all(bf16[16,32,2048]{2,1,0:T(8,128)(2,1)S(1)} %stack.18), channel_id=1, replica_groups=mesh['section'=16,'tp'=16] {'tp'}, dimensions={0} | all-to-all | bytes 4194304 | tf_op jit(solution)/shard_map/all_to_all | solution.py:68
  249.2 2.4 collective-permute-done.6
  251.6 0.7 convolution_add_fusion.3
  252.3 0.7 fusion.4
  254.3 4.0 collective-permute-done.7
  258.3 2.1 add_convert_fusion.1
  260.5 95.5 %reduce-scatter.6.cloned.1.call-done = bf16[32,2048]{1,0:T(8,128)(2,1)} async-done(((bf16[512,2048]{1,0:T(8,128)(2,1)}), bf16[32,2048]{1,0:T(8,128)(2,1)}) %reduce-scatter.6.cloned.1.call-update) | async-done | bytes 131088 | tf_op jit(solution)/shard_map/reduce_scatter | solution.py:95
  356.0 0.9 collective-permute-start.8
  356.8 4.8 collective-permute-done.8
  361.6 0.9 add_convert_fusion.5
  362.6 1.1 collective-permute-start.9
  363.7 5.5 collective-permute-done.9
  369.2 1.7 collective-permute-start.10
  370.9 2.5 collective-permute-done.10
  373.6 1.1 collective-permute-done.11
  375.1 49.0 %all_to_all.17 = bf16[16,32,2048]{2,1,0:T(8,128)(2,1)S(1)} all-to-all(bf16[16,32,2048]{2,1,0:T(8,128)(2,1)S(1)} %stack.20), channel_id=1, replica_groups=mesh['section'=16,'tp'=16] {'tp'}, dimensions={0} | all-to-all | bytes 4194304 | tf_op jit(solution)/shard_map/all_to_all | solution.py:68
  425.9 2.4 collective-permute-done.12
  429.0 0.7 fusion.5
  431.0 4.0 collective-permute-done.13
  435.0 2.1 add_convert_fusion
  437.1 95.5 %reduce-scatter.8.cloned.1.call-done = bf16[32,2048]{1,0:T(8,128)(2,1)} async-done(((bf16[512,2048]{1,0:T(8,128)(2,1)}), bf16[32,2048]{1,0:T(8,128)(2,1)}) %reduce-scatter.8.cloned.1.call-update) | async-done | bytes 131088 | tf_op jit(solution)/shard_map/reduce_scatter | solution.py:95
  532.6 0.9 collective-permute-start.14
  533.5 4.7 collective-permute-done.14
  538.2 0.9 add_convert_fusion.3
  539.2 1.1 collective-permute-start.15
  540.5 5.2 collective-permute-done.15
  (84 shorter events, 12.1 us)
Async XLA Ops:
  6.5 5.6 %copy-start = (f32[2,4096]{1,0:T(2,128)S(1)}, f32[2,4096]{1,0:T(2,128)}, u32[]{:S(2)}) copy-start(f32[2,4096]{1,0:T(2,128)} %param.6) | copy-start | bytes 98308
  6.5 172.8 %reduce-scatter.4.cloned.1.call-start = ((), (), s32[]{:S(2)}) async-start(), calls=%async_computation.6 | async-start | bytes 2228224 | tf_op jit(solution)/shard_map/reduce_scatter | solution.py:95
  12.6 61.3 %copy-start.10 = (bf16[1,128,4096]{2,1,0:T(8,128)(2,1)S(1)}, bf16[1,128,4096]{2,1,0:T(8,128)(2,1)}, u32[]{:S(2)}) copy-start(bf16[1,128,4096]{2,1,0:T(8,128)(2,1)} %param.9) | copy-start | bytes 3145732
  73.8 6.0 %collective-permute-start = (bf16[512,2048]{1,0:T(8,128)(2,1)S(1)}, bf16[512,2048]{1,0:T(8,128)(2,1)}, u32[]{:S(2)}, u32[]{:S(2)}) collective-permute-start(bf16[512,2048]{1,0:T(8,128)(2,1)S(1)} %bitcast.76), channel_id=1, source_target_pairs={{0,16},{16,0},{32,48},{48,32},{64,80},{80,64},{96,112},{112,96},{1... | collective-permute-start | bytes 6291464 | tf_op jit(solution)/shard_map/ppermute | solution.py:13
  76.4 8.0 %copy-start.7 = (bf16[128,4,1,512]{0,3,2,1:T(8,128)(2,1)}, bf16[128,4,1,512]{0,3,2,1:T(8,128)(2,1)S(1)}, u32[]{:S(2)}) copy-start(bf16[128,4,1,512]{0,3,2,1:T(8,128)(2,1)S(1)} %get-tuple-element.8) | copy-start | bytes 1572868
  78.3 1.5 copy-start.1
  78.3 1.5 copy-start.4
  78.3 3.8 copy-start.12
  85.2 4.4 collective-permute-start.1
  91.6 105.3 %copy-start.11 = (f32[32,4,512]{2,1,0:T(4,128)S(1)}, f32[32,4,512]{2,1,0:T(4,128)}, u32[]{:S(2)}) copy-start(f32[32,4,512]{2,1,0:T(4,128)} %get-tuple-element.17) | copy-start | bytes 786436
  91.6 264.4 %reduce-scatter.6.cloned.1.call-start = ((), (), s32[]{:S(2)}) async-start(), calls=%async_computation.7 | async-start | bytes 2228224 | tf_op jit(solution)/shard_map/reduce_scatter | solution.py:95
  179.4 5.7 %collective-permute-start.2 = (bf16[32,2048]{1,0:T(8,128)(2,1)}, bf16[32,2048]{1,0:T(8,128)(2,1)S(1)}, u32[]{:S(2)}, u32[]{:S(2)}) collective-permute-start(bf16[32,2048]{1,0:T(8,128)(2,1)} %reduce-scatter.4.cloned.1.call-done), channel_id=1, source_target_pairs={{0,32},{16,48},{32,0},{48,16},{64,96},{80,112},{96,64},{112,80},{1... | collective-permute-start | bytes 393224 | tf_op jit(solution)/shard_map/ppermute | solution.py:13
  186.0 6.6 %collective-permute-start.3 = (bf16[32,2048]{1,0:T(8,128)(2,1)S(1)}, bf16[32,2048]{1,0:T(8,128)(2,1)S(1)}, u32[]{:S(2)}, u32[]{:S(2)}) collective-permute-start(bf16[32,2048]{1,0:T(8,128)(2,1)S(1)} %add_convert_fusion.7), channel_id=1, source_target_pairs={{0,64},{16,80},{32,96},{48,112},{64,0},{80,16},{96,32},{112,48},{1... | collective-permute-start | bytes 393224 | tf_op jit(solution)/shard_map/ppermute | solution.py:13
  192.6 4.1 collective-permute-start.4
  196.8 1.2 collective-permute-start.5
  198.4 49.0 %copy-start.5 = (bf16[4,1,512,128]{3,2,1,0:T(8,128)(2,1)S(1)}, bf16[4,1,512,128]{3,2,1,0:T(8,128)(2,1)}, u32[]{:S(2)}) copy-start(bf16[4,1,512,128]{3,2,1,0:T(8,128)(2,1)} %copy-done.4) | copy-start | bytes 1572868
  247.4 1.0 copy-start.2
  247.4 4.2 collective-permute-start.6
  249.2 3.1 copy-start.13
  252.3 1.0 copy-start.8
  254.1 4.2 collective-permute-start.7
  260.4 272.2 %reduce-scatter.8.cloned.1.call-start = ((), (), s32[]{:S(2)}) async-start(), calls=%async_computation.8 | async-start | bytes 2228224 | tf_op jit(solution)/shard_map/reduce_scatter | solution.py:95
  356.0 5.6 %collective-permute-start.8 = (bf16[32,2048]{1,0:T(8,128)(2,1)}, bf16[32,2048]{1,0:T(8,128)(2,1)S(1)}, u32[]{:S(2)}, u32[]{:S(2)}) collective-permute-start(bf16[32,2048]{1,0:T(8,128)(2,1)} %reduce-scatter.6.cloned.1.call-done), channel_id=1, source_target_pairs={{0,32},{16,48},{32,0},{48,16},{64,96},{80,112},{96,64},{112,80},{1... | collective-permute-start | bytes 393224 | tf_op jit(solution)/shard_map/ppermute | solution.py:13
  362.6 6.6 %collective-permute-start.9 = (bf16[32,2048]{1,0:T(8,128)(2,1)S(1)}, bf16[32,2048]{1,0:T(8,128)(2,1)S(1)}, u32[]{:S(2)}, u32[]{:S(2)}) collective-permute-start(bf16[32,2048]{1,0:T(8,128)(2,1)S(1)} %add_convert_fusion.5), channel_id=1, source_target_pairs={{0,64},{16,80},{32,96},{48,112},{64,0},{80,16},{96,32},{112,48},{1... | collective-permute-start | bytes 393224 | tf_op jit(solution)/shard_map/ppermute | solution.py:13
  369.2 4.2 collective-permute-start.10
  373.5 1.2 collective-permute-start.11
  375.1 49.1 %copy-start.6 = (bf16[4,1,512,128]{3,2,1,0:T(8,128)(2,1)S(1)}, bf16[4,1,512,128]{3,2,1,0:T(8,128)(2,1)}, u32[]{:S(2)}) copy-start(bf16[4,1,512,128]{3,2,1,0:T(8,128)(2,1)} %copy-done.4) | copy-start | bytes 1572868
  424.2 1.0 copy-start.3
  424.2 4.2 collective-permute-start.12
  429.0 1.0 copy-start.9
  430.8 4.2 collective-permute-start.13
  532.6 5.6 %collective-permute-start.14 = (bf16[32,2048]{1,0:T(8,128)(2,1)}, bf16[32,2048]{1,0:T(8,128)(2,1)S(1)}, u32[]{:S(2)}, u32[]{:S(2)}) collective-permute-start(bf16[32,2048]{1,0:T(8,128)(2,1)} %reduce-scatter.8.cloned.1.call-done), channel_id=1, source_target_pairs={{0,32},{16,48},{32,0},{48,16},{64,96},{80,112},{96,64},{112,80},{1... | collective-permute-start | bytes 393224 | tf_op jit(solution)/shard_map/ppermute | solution.py:13
  539.2 6.6 %collective-permute-start.15 = (bf16[32,2048]{1,0:T(8,128)(2,1)S(1)}, bf16[32,2048]{1,0:T(8,128)(2,1)S(1)}, u32[]{:S(2)}, u32[]{:S(2)}) collective-permute-start(bf16[32,2048]{1,0:T(8,128)(2,1)S(1)} %add_convert_fusion.3), channel_id=1, source_target_pairs={{0,64},{16,80},{32,96},{48,112},{64,0},{80,16},{96,32},{112,48},{1... | collective-permute-start | bytes 393224 | tf_op jit(solution)/shard_map/ppermute | solution.py:13
Sparse Core Ops, SparseCore 0:
  91.8 87.5 reduce-scatter.3
  260.5 95.3 reduce-scatter.5
  437.2 95.3 reduce-scatter.7
